TPU v7x, 512 devices: a whole 4x8x8 slice. The times are simulated.
512 devices in a mesh: col: 64 (over z_lo, y, core), row: 8 (over x, z_hi).
Axes of the slice: x: 4, y: 8, z: 8 (z_hi: 2, z_lo: 4; z = z_hi * 4 + z_lo), core: 2. Of those that a mesh axis runs over, the one named last changes fastest.
Arguments:
- image: bfloat16 [96, 64, 8192], P(None, 'row', 'col'), may hold values from -6 to 6
- cotangent: bfloat16 [96, 64, 8192], P(None, 'row', 'col'), may hold values from -6 to 6
- dw_kernel: float32 [96, 7, 7], replicated, may hold values from -0.875 to 0.875
- dw_bias: float32 [96], replicated, may hold values from -3 to 3
- ln_gain: float32 [96], replicated, may hold values from 0.1 to 1.9
- ln_bias: float32 [96], replicated, may hold values from -3 to 3
- w_in: bfloat16 [96, 384], replicated, may hold values from -0.625 to 0.625
- b_in: float32 [384], replicated, may hold values from -3 to 3
- w_out: bfloat16 [384, 96], replicated, may hold values from -0.3125 to 0.3125
- layer_scale: float32 [96], replicated, may hold values from 0.5 to 2
Outputs:
- block_out: bfloat16 [96, 64, 8192], P(None, 'row', 'col')
- image_grad: bfloat16 [96, 64, 8192], P(None, 'row', 'col')
- kernel_grad: float32 [96, 7, 7], replicated
- dw_bias_grad: float32 [96], replicated
- gain_grad: float32 [96], replicated
- ln_bias_grad: float32 [96], replicated
- w_in_grad: float32 [96, 384], replicated
- b_in_grad: float32 [384], replicated
- w_out_grad: float32 [384, 96], replicated
- scale_grad: float32 [96], replicated
All inputs are finite; a program needn't handle non-finite values.
Results may differ from a plain program's by a relative error of at most 0.0065.
Values may be sent and summed in bfloat16 or wider, within the bound.
No kernel may reach another device: no remote copies, remote signals or barrier semaphores. Data moves between devices by JAX's collectives and lax.ppermute only.
A program may use at most 64 MiB of HBM per device.

v0:
```python
import math
import jax
import jax.numpy as jnp
from jax import lax
from jax.sharding import PartitionSpec as P


def padded_2(block, sides, width):
    for axis, dim in sides:
        count = lax.axis_size(axis)
        forward = [(i, i + 1) for i in range(count - 1)]
        backward = [(target, source) for source, target in forward]
        low = lax.ppermute(
            lax.slice_in_dim(block, block.shape[dim] - width, None, axis=dim), axis, forward
        )
        high = lax.ppermute(lax.slice_in_dim(block, 0, width, axis=dim), axis, backward)
        block = jnp.concatenate([low, block, high], axis=dim)
    return block


def from_behind(value, axis, steps):
    count = lax.axis_size(axis)
    initial, last = (max(0, -steps), min(count, count - steps))
    return lax.ppermute(value, axis, [(source, source + steps) for source in range(initial, last)])


def conv_seven(padded, kernel):
    height = padded.shape[1] - 6
    breadth = padded.shape[2] - 6
    summed = jnp.zeros((padded.shape[0], height, breadth), jnp.float32)
    for row_step in range(7):
        for col_step in range(7):
            summed = (
                summed
                + kernel[:, row_step, col_step][:, None, None]
                * padded[:, row_step : row_step + height, col_step : col_step + breadth]
            )
    return summed


def kernel_terms(conv_grad, padded):
    height, breadth = (conv_grad.shape[1], conv_grad.shape[2])
    pieces = []
    for row_step in range(7):
        for col_step in range(7):
            pieces.append(
                jnp.sum(
                    conv_grad
                    * padded[:, row_step : row_step + height, col_step : col_step + breadth],
                    axis=(1, 2),
                )
            )
    return jnp.stack(pieces, axis=1).reshape(conv_grad.shape[0], 7, 7)


def product(form, left, right):
    return jnp.einsum(form, left, right, preferred_element_type=jnp.float32)


def mixing(conv_flat, image_flat, cotan_flat, ln_gain, ln_bias, w_in, b_in, w_out, layer_scale):
    average = jnp.mean(conv_flat, axis=0, keepdims=True)
    centred = conv_flat - average
    spread = jnp.mean(centred * centred, axis=0, keepdims=True)
    inverse = lax.rsqrt(spread + 1e-06)
    normed = centred * inverse
    ln_out = (normed * ln_gain[:, None] + ln_bias[:, None]).astype(jnp.bfloat16)
    pre_act = product("ch,cp->hp", w_in, ln_out) + b_in[:, None]
    act_out, gelu_pull = jax.vjp(jax.nn.gelu, pre_act)
    activ = act_out.astype(jnp.bfloat16)
    branch = product("hc,hp->cp", w_out, activ)
    scale_col = layer_scale[:, None]
    block_out = (image_flat.astype(jnp.float32) + scale_col * branch).astype(jnp.bfloat16)
    upstream = cotan_flat.astype(jnp.float32)
    scale_sum = jnp.sum(upstream * branch, axis=1)
    branch_grad = (scale_col * upstream).astype(jnp.bfloat16)
    w_out_sum = product("hp,cp->hc", activ, branch_grad)
    act_grad = product("hc,cp->hp", w_out, branch_grad)
    pre_grad = gelu_pull(act_grad)[0].astype(jnp.bfloat16)
    b_in_sum = jnp.sum(pre_grad.astype(jnp.float32), axis=1)
    w_in_sum = product("cp,hp->ch", ln_out, pre_grad)
    ln_grad = product("ch,hp->cp", w_in, pre_grad)
    gain_sum = jnp.sum(ln_grad * normed, axis=1)
    shift_sum = jnp.sum(ln_grad, axis=1)
    normed_grad = ln_grad * ln_gain[:, None]
    conv_grad = inverse * (
        normed_grad
        - jnp.mean(normed_grad, axis=0, keepdims=True)
        - normed * jnp.mean(normed_grad * normed, axis=0, keepdims=True)
    )
    return (block_out, conv_grad, (gain_sum, shift_sum, w_in_sum, b_in_sum, w_out_sum, scale_sum))


def local(image, cotangent, dw_kernel, dw_bias, ln_gain, ln_bias, w_in, b_in, w_out, layer_scale):
    channels, height, breadth = image.shape
    pixels = height * breadth
    padded = padded_2(image, (("col", 2), ("row", 1)), 3)
    conv_out = conv_seven(padded, dw_kernel) + dw_bias[:, None, None]
    block_flat, grad_flat, sums = mixing(
        conv_out.reshape(channels, pixels),
        image.reshape(channels, pixels),
        cotangent.reshape(channels, pixels),
        ln_gain,
        ln_bias,
        w_in,
        b_in,
        w_out,
        layer_scale,
    )
    gain_sum, shift_sum, w_in_sum, b_in_sum, w_out_sum, scale_sum = sums
    block_out = block_flat.reshape(channels, height, breadth)
    conv_grad = grad_flat.reshape(channels, height, breadth)
    flipped = dw_kernel[:, ::-1, ::-1]
    extended = conv_seven(jnp.pad(conv_grad, ((0, 0), (6, 6), (6, 6))), flipped)
    from_above = from_behind(extended[:, height + 3 :, :].astype(jnp.bfloat16), "row", 1).astype(
        jnp.float32
    )
    from_below = from_behind(extended[:, :3, :].astype(jnp.bfloat16), "row", -1).astype(jnp.float32)
    middle = extended[:, 3 : height + 3, :]
    middle = middle.at[:, :3, :].add(from_above)
    middle = middle.at[:, height - 3 :, :].add(from_below)
    from_left = from_behind(middle[:, :, breadth + 3 :], "col", 1)
    from_right = from_behind(middle[:, :, :3], "col", -1)
    back = middle[:, :, 3 : breadth + 3]
    back = back.at[:, :, :3].add(from_left)
    back = back.at[:, :, breadth - 3 :].add(from_right)
    image_grad = (cotangent.astype(jnp.float32) + back).astype(jnp.bfloat16)
    kernel_sum = kernel_terms(conv_grad, padded)
    bias_sum = jnp.sum(conv_grad, axis=(1, 2))
    kernel_sum, bias_sum, gain_sum, shift_sum, w_in_sum, b_in_sum, w_out_sum, scale_sum = lax.psum(
        (kernel_sum, bias_sum, gain_sum, shift_sum, w_in_sum, b_in_sum, w_out_sum, scale_sum),
        ("col", "row"),
    )
    factor = 1.0 / math.sqrt(height * lax.axis_size("row") * breadth * lax.axis_size("col"))
    return (
        block_out,
        image_grad,
        factor * kernel_sum,
        factor * bias_sum,
        factor * gain_sum,
        factor * shift_sum,
        factor * w_in_sum,
        factor * b_in_sum,
        factor * w_out_sum,
        factor * scale_sum,
    )


def solution(mesh):
    in_specs = (
        P(None, "row", "col"),
        P(None, "row", "col"),
        P(),
        P(),
        P(),
        P(),
        P(),
        P(),
        P(),
        P(),
    )
    out_specs = (
        P(None, "row", "col"),
        P(None, "row", "col"),
        P(),
        P(),
        P(),
        P(),
        P(),
        P(),
        P(),
        P(),
    )
    return jax.shard_map(local, mesh=mesh, in_specs=in_specs, out_specs=out_specs, check_vma=False)
```

profile of v0, /device:TPU:1, one launch (start us, length us, event | category | flops | bytes accessed | tf_op | source)
XLA Modules:
  0.0 492.2 jit_solution(10161626249035542997)
XLA Ops:
  8.4 4.6 collective-permute-start
  13.0 5.5 %collective-permute-start.1 = (bf16[96,8,3]{0,2,1:T(4,128)(2,1)S(1)}, bf16[96,8,3]{0,2,1:T(4,128)(2,1)S(1)}, u32[]{:S(2)}, u32[]{:S(2)}) collective-permute-start(bf16[96,8,3]{0,2,1:T(4,128)(2,1)S(1)} %get-tuple-element.145), channel_id=1, source_target_pairs={{8,0},{16,8},{24,16},{32,24},{40,32},{48,40},{56,48},{64,56},{72,6... | collective-permute-start | bytes 13832 | tf_op jit(solution)/shard_map/ppermute | solution.py:16
  20.6 8.1 %collective-permute-start.2 = (bf16[96,3,134]{0,2,1:T(8,128)(2,1)S(1)}, bf16[96,3,134]{0,2,1:T(8,128)(2,1)S(1)}, u32[]{:S(2)}, u32[]{:S(2)}) collective-permute-start(bf16[96,3,134]{0,2,1:T(8,128)(2,1)S(1)} %get-tuple-element.142), channel_id=1, source_target_pairs={{0,1},{1,2},{2,3},{3,4},{4,5},{5,6},{6,7},{8,9},{9,10},{10,11},{11... | collective-permute-start | bytes 231560 | tf_op jit(solution)/shard_map/ppermute | solution.py:13
  32.8 7.5 %collective-permute-done.3 = bf16[96,3,134]{0,2,1:T(8,128)(2,1)S(1)} collective-permute-done((bf16[96,3,134]{0,2,1:T(8,128)(2,1)S(1)}, bf16[96,3,134]{0,2,1:T(8,128)(2,1)S(1)}, u32[]{:S(2)}, u32[]{:S(2)}) %collective-permute-start.3) | collective-permute-done | bytes 77216 | tf_op jit(solution)/shard_map/ppermute | solution.py:16
  40.5 4.3 fusion.223
  45.4 1.7 fusion.107
  47.1 2.0 convert_reduce_fusion
  51.1 1.9 fusion.203
  53.0 1.9 fusion.153
  55.8 23.9 %fusion.221 = (bf16[96,14,134]{2,1,0:T(8,128)(2,1)}, f32[96,14,134]{2,1,0:T(8,128)S(1)}) fusion(f32[96]{0:T(128)S(1)} %get-tuple-element.146, f32[96]{0:T(128)S(1)} %get-tuple-element.165, f32[96]{0:T(128)S(1)} %get-tuple-element.184, f32[96]{0:T(128)S(1)} %get-tuple-element.192, f32[96]{0:T(128)S(1)} %get-tuple-element.191, f32[96]{0:T(128)S(1)} %get-tuple-element.190, ...), kind=kLoop, calls=%fused_computation.460 | loop fusion | flops 17649408 | bytes 1492608 | tf_op jit(solution)/shard_map/convert.3
  82.6 1.9 fusion.206
  84.5 100.3 %all-reduce.1 = (f32[96,7,7]{0,2,1:T(8,128)S(1)}, f32[96]{0:T(128)S(1)}, f32[96]{0:T(128)S(1)}, f32[96]{0:T(128)S(1)}, f32[384]{0:T(512)S(1)}, /*index=5*/f32[96]{0:T(128)S(1)}) all-reduce(f32[96,7,7]{0,2,1:T(8,128)S(1)} %reshape.203, f32[96]{0:T(128)S(1)} %get-tuple-element.101, ...), channel_id=1, replica_groups=mesh['col'=64,'row'=8] {'col','row'}, use_global_device_ids=true, to_apply=%region_53.54 | all-reduce | flops 5472 | bytes 43776 | tf_op jit(solution)/shard_map/psum | solution.py:129
  187.2 3.4 collective-permute-start.4
  192.6 3.4 collective-permute-done.4
  196.1 2.6 scatter-add.14
  198.7 8.0 %collective-permute-done.5 = bf16[96,3,134]{2,1,0:T(4,128)(2,1)S(1)} collective-permute-done((bf16[96,3,134]{2,1,0:T(4,128)(2,1)S(1)}, bf16[96,3,134]{2,1,0:T(4,128)(2,1)S(1)}, u32[]{:S(2)}, u32[]{:S(2)}) %collective-permute-start.5) | collective-permute-done | bytes 77216 | tf_op jit(solution)/shard_map/ppermute | solution.py:24
  206.8 2.6 scatter-add.15
  209.5 4.8 collective-permute-start.6
  215.7 1.9 collective-permute-start.7
  219.2 6.1 %scatter-add.16 = f32[96,8,128]{2,1,0:T(8,128)S(1)} dynamic-update-slice(f32[96,8,128]{2,1,0:T(8,128)S(1)} %slice.979, f32[96,8,3]{2,1,0:T(8,128)S(1)} %slice_add_fusion.1, s32[]{:T(128)} %constant.134.clone.1, s32[]{:T(128)} %constant.134.clone.1, s32[]{:T(128)} %constant.134.clone.1) | dynamic-update-slice | bytes 18436 | tf_op jit(solution)/shard_map/scatter-add | solution.py:124
  225.4 18.6 %scatter-add.19 = f32[96,8,128]{2,1,0:T(8,128)S(1)} dynamic-update-slice(f32[96,8,128]{2,1,0:T(8,128)S(1)} %scatter-add.16, f32[96,8,3]{2,1,0:T(8,128)S(1)} %slice_add_fusion, s32[]{:T(128)} %constant.134.clone.1, s32[]{:T(128)} %constant.134.clone.1, s32[]{:T(128)} %constant.136.clone.1) | dynamic-update-slice | bytes 18436 | tf_op jit(solution)/shard_map/scatter-add | solution.py:125
  244.7 237.4 %all-reduce.5.cloned.1.call-done = (f32[96,384]{1,0:T(8,128)}, f32[384,96]{0,1:T(8,128)}) async-done(((f32[96,384]{1,0:T(8,128)}, f32[384,96]{0,1:T(8,128)}), (f32[96,384]{1,0:T(8,128)}, f32[384,96]{0,1:T(8,128)})) %all-reduce.5.cloned.1.call-update) | async-done | bytes 294928 | tf_op jit(solution)/shard_map/psum | solution.py:129
  482.2 1.6 broadcast_multiply_fusion
  483.8 1.6 broadcast_multiply_fusion.1
  (138 shorter events, 21.9 us)
Async XLA Ops:
  7.2 38.2 %copy-start = (bf16[96,384]{1,0:T(8,128)(2,1)S(1)}, bf16[96,384]{1,0:T(8,128)(2,1)}, u32[]{:S(2)}) copy-start(bf16[96,384]{1,0:T(8,128)(2,1)} %param.24) | copy-start | bytes 221188
  7.2 475.0 %all-reduce.5.cloned.1.call-start = ((), (), s32[]{:S(2)}) async-start(), calls=%async_computation | async-start | bytes 589824 | tf_op jit(solution)/shard_map/psum | solution.py:129
  8.4 32.1 %copy-start.41 = (f32[96]{0:T(128)S(1)}, f32[96]{0:T(128)}, u32[]{:S(2)}) copy-start(f32[96]{0:T(128)} %param.21) | copy-start | bytes 1156
  8.4 12.1 %collective-permute-start = (bf16[96,8,3]{0,2,1:T(4,128)(2,1)S(1)}, bf16[96,8,3]{0,2,1:T(4,128)(2,1)S(1)}, u32[]{:S(2)}, u32[]{:S(2)}) collective-permute-start(bf16[96,8,3]{0,2,1:T(4,128)(2,1)S(1)} %get-tuple-element.144), channel_id=1, source_target_pairs={{0,8},{8,16},{16,24},{24,32},{32,40},{40,48},{48,56},{56,64},{64,7... | collective-permute-start | bytes 13832 | tf_op jit(solution)/shard_map/ppermute | solution.py:13
  13.0 7.5 %collective-permute-start.1 = (bf16[96,8,3]{0,2,1:T(4,128)(2,1)S(1)}, bf16[96,8,3]{0,2,1:T(4,128)(2,1)S(1)}, u32[]{:S(2)}, u32[]{:S(2)}) collective-permute-start(bf16[96,8,3]{0,2,1:T(4,128)(2,1)S(1)} %get-tuple-element.145), channel_id=1, source_target_pairs={{8,0},{16,8},{24,16},{32,24},{40,32},{48,40},{56,48},{64,56},{72,6... | collective-permute-start | bytes 13832 | tf_op jit(solution)/shard_map/ppermute | solution.py:16
  20.6 12.2 %collective-permute-start.2 = (bf16[96,3,134]{0,2,1:T(8,128)(2,1)S(1)}, bf16[96,3,134]{0,2,1:T(8,128)(2,1)S(1)}, u32[]{:S(2)}, u32[]{:S(2)}) collective-permute-start(bf16[96,3,134]{0,2,1:T(8,128)(2,1)S(1)} %get-tuple-element.142), channel_id=1, source_target_pairs={{0,1},{1,2},{2,3},{3,4},{4,5},{5,6},{6,7},{8,9},{9,10},{10,11},{11... | collective-permute-start | bytes 231560 | tf_op jit(solution)/shard_map/ppermute | solution.py:13
  28.7 11.6 %collective-permute-start.3 = (bf16[96,3,134]{0,2,1:T(8,128)(2,1)S(1)}, bf16[96,3,134]{0,2,1:T(8,128)(2,1)S(1)}, u32[]{:S(2)}, u32[]{:S(2)}) collective-permute-start(bf16[96,3,134]{0,2,1:T(8,128)(2,1)S(1)} %get-tuple-element.143), channel_id=1, source_target_pairs={{1,0},{2,1},{3,2},{4,3},{5,4},{6,5},{7,6},{9,8},{10,9},{11,10},{12... | collective-permute-start | bytes 231560 | tf_op jit(solution)/shard_map/ppermute | solution.py:16
  31.9 15.3 %copy-start.3 = (f32[12,8,8,128]{3,2,1,0:T(8,128)}, f32[12,8,8,128]{3,2,1,0:T(8,128)S(1)}, u32[]{:S(2)}) copy-start(f32[12,8,8,128]{3,2,1,0:T(8,128)S(1)} %convert.8) | copy-start | bytes 1179652
  40.5 4.9 copy-start.9
  40.5 4.9 copy-start.42
  40.5 4.9 copy-start.43
  55.8 24.2 %copy-start.4 = (f32[12,8,8,128]{3,2,1,0:T(8,128)S(1)}, f32[12,8,8,128]{3,2,1,0:T(8,128)}, u32[]{:S(2)}) copy-start(f32[12,8,8,128]{3,2,1,0:T(8,128)} %copy-done.3) | copy-start | bytes 1179652
  55.8 24.2 %copy-start.5 = (bf16[384,1024]{0,1:T(8,128)(2,1)S(1)}, bf16[384,1024]{0,1:T(8,128)(2,1)}, u32[]{:S(2)}) copy-start(bf16[384,1024]{0,1:T(8,128)(2,1)} %get-tuple-element.197) | copy-start | bytes 2359300
  79.8 2.3 copy-start.14
  79.8 2.3 copy-start.15
  79.8 2.3 copy-start.16
  79.8 2.3 copy-start.17
  82.0 2.4 copy-start.40
  82.0 105.0 %copy-start.6 = (bf16[96,14,134]{2,1,0:T(8,128)(2,1)S(1)}, bf16[96,14,134]{2,1,0:T(8,128)(2,1)}, u32[]{:S(2)}) copy-start(bf16[96,14,134]{2,1,0:T(8,128)(2,1)} %get-tuple-element.129) | copy-start | bytes 1080580
  187.2 8.8 %collective-permute-start.4 = (bf16[96,3,134]{2,1,0:T(4,128)(2,1)S(1)}, bf16[96,3,134]{2,1,0:T(4,128)(2,1)S(1)}, u32[]{:S(2)}, u32[]{:S(2)}) collective-permute-start(bf16[96,3,134]{2,1,0:T(4,128)(2,1)S(1)} %get-tuple-element.137), channel_id=1, source_target_pairs={{0,1},{1,2},{2,3},{3,4},{4,5},{5,6},{6,7},{8,9},{9,10},{10,11},{11... | collective-permute-start | bytes 231560 | tf_op jit(solution)/shard_map/ppermute | solution.py:24
  191.3 15.4 %collective-permute-start.5 = (bf16[96,3,134]{2,1,0:T(4,128)(2,1)S(1)}, bf16[96,3,134]{2,1,0:T(4,128)(2,1)S(1)}, u32[]{:S(2)}, u32[]{:S(2)}) collective-permute-start(bf16[96,3,134]{2,1,0:T(4,128)(2,1)S(1)} %get-tuple-element.136), channel_id=1, source_target_pairs={{1,0},{2,1},{3,2},{4,3},{5,4},{6,5},{7,6},{9,8},{10,9},{11,10},{12... | collective-permute-start | bytes 231560 | tf_op jit(solution)/shard_map/ppermute | solution.py:24
  209.5 9.5 %collective-permute-start.6 = (f32[96,8,3]{2,1,0:T(8,128)S(1)}, f32[96,8,3]{2,1,0:T(8,128)S(1)}, u32[]{:S(2)}, u32[]{:S(2)}) collective-permute-start(f32[96,8,3]{2,1,0:T(8,128)S(1)} %get-tuple-element.135), channel_id=1, source_target_pairs={{0,8},{8,16},{16,24},{24,32},{32,40},{40,48},{48,56},{56,64},{64,7... | collective-permute-start | bytes 27656 | tf_op jit(solution)/shard_map/ppermute | solution.py:24
  215.7 9.6 %collective-permute-start.7 = (f32[96,8,3]{2,1,0:T(8,128)S(1)}, f32[96,8,3]{2,1,0:T(8,128)S(1)}, u32[]{:S(2)}, u32[]{:S(2)}) collective-permute-start(f32[96,8,3]{2,1,0:T(8,128)S(1)} %get-tuple-element.134), channel_id=1, source_target_pairs={{8,0},{16,8},{24,16},{32,24},{40,32},{48,40},{56,48},{64,56},{72,6... | collective-permute-start | bytes 27656 | tf_op jit(solution)/shard_map/ppermute | solution.py:24
  219.1 24.9 %copy-start.7 = (bf16[96,8,128]{2,1,0:T(8,128)(2,1)S(1)}, bf16[96,8,128]{2,1,0:T(8,128)(2,1)}, u32[]{:S(2)}) copy-start(bf16[96,8,128]{2,1,0:T(8,128)(2,1)} %param.19) | copy-start | bytes 589828
  (29 other events, 64.0 us)
Sparse Core Ops, SparseCore 0:
  215.6 266.4 all-reduce.4
where the time goes:
time: 493 us; the launch traced here: 492 us
  waiting for transfers between devices  258 us (52%)
  blocking collectives  100 us (20%)
  other arithmetic  43.3 us (9%)
  local copies, waits for them, and re-layouts  37.1 us (8%)
  starting transfers between devices  30.9 us (6%)
  between operations  14.9 us (3%)
  matrix products  7.92 us (2%)
    psum x1, waiting for transfers between devices, local(): lax.psum((kernel_sum, bias_sum, gain_sum, shift_sum, w_in_sum, b_in_sum,...  237 us
    psum x1, blocking collectives, local(): lax.psum((kernel_sum, bias_sum, gain_sum, shift_sum, w_in_sum, b_in_sum,...  100 us
    another operation x1, other arithmetic  23.9 us
    scatter-add x1, local copies, waits for them, and re-layouts, local(): back = back.at[:, :, breadth - 3:].add(from_right)  18.6 us
    ppermute x4, waiting for transfers between devices, from_behind(): lax.ppermute(value, axis, [(source, source + steps) for source in range(i...  12.7 us
    ppermute x2, starting transfers between devices, padded_2(): lax.ppermute(lax.slice_in_dim(block, block.shape[dim] - width, None, axis...  12.7 us
    ppermute x4, starting transfers between devices, from_behind(): lax.ppermute(value, axis, [(source, source + steps) for source in range(i...  11.4 us
  transfers between devices with their start and end apart: 9, of which 5 were waited for; matrix products, arithmetic and copies ran while one was open for 7% of the time, Pallas kernels for 0%

commit v1 on v0

--- a/solution.py
+++ b/solution.py
@@ -127,8 +127,11 @@
     kernel_sum = kernel_terms(conv_grad, padded)
     bias_sum = jnp.sum(conv_grad, axis=(1, 2))
     kernel_sum, bias_sum, gain_sum, shift_sum, w_in_sum, b_in_sum, w_out_sum, scale_sum = lax.psum(
-        (kernel_sum, bias_sum, gain_sum, shift_sum, w_in_sum, b_in_sum, w_out_sum, scale_sum),
-        ("col", "row"),
+        lax.psum(
+            (kernel_sum, bias_sum, gain_sum, shift_sum, w_in_sum, b_in_sum, w_out_sum, scale_sum),
+            "col",
+        ),
+        "row",
     )
     factor = 1.0 / math.sqrt(height * lax.axis_size("row") * breadth * lax.axis_size("col"))
     return (

time: 493 us -> 1030 us (2.09)
  waiting for transfers between devices: 258 us -> 570 us
  blocking collectives: 100 us -> 304 us
  starting transfers between devices: 30.9 us -> 41.4 us
    psum x1, waiting for transfers between devices: 237 us -> 467 us  [local(): lax.psum((kernel_sum, bias_sum, gain_sum, shift_sum, w_in_sum, b_in_sum,...]
    psum x1, blocking collectives: 100 us -> 261 us  [local(): lax.psum((kernel_sum, bias_sum, gain_sum, shift_sum, w_in_sum, b_in_sum,...]
    psum x0 -> x1, waiting for transfers between devices: none -> 89.8 us  [local(): lax.psum(lax.psum((kernel_sum, bias_sum, gain_sum, shift_sum, w_in_sum, b...]
    psum x0 -> x1, blocking collectives: none -> 42.8 us  [local(): lax.psum(lax.psum((kernel_sum, bias_sum, gain_sum, shift_sum, w_in_sum, b...]
    ppermute x4, starting transfers between devices: 11.4 us -> 21.9 us  [from_behind(): lax.ppermute(value, axis, [(source, source + steps) for source in range(i...]
  transfers between devices with their start and end apart: 9 -> 10, of which waited for: 5 -> 5; matrix products, arithmetic and copies ran while one was open for 7% -> 4% of each run, Pallas kernels for 0% -> 0%
where the time goes in v1:
time: 1030 us; the launch traced here: 1020 us
  waiting for transfers between devices  570 us (55%)
  blocking collectives  304 us (30%)
  other arithmetic  45.6 us (4%)
  starting transfers between devices  41.4 us (4%)
  local copies, waits for them, and re-layouts  39.9 us (4%)
  between operations  15.6 us (2%)
    psum x1, waiting for transfers between devices, local(): lax.psum((kernel_sum, bias_sum, gain_sum, shift_sum, w_in_sum, b_in_sum,...  467 us
    psum x1, blocking collectives, local(): lax.psum((kernel_sum, bias_sum, gain_sum, shift_sum, w_in_sum, b_in_sum,...  261 us
    psum x1, waiting for transfers between devices, local(): lax.psum(lax.psum((kernel_sum, bias_sum, gain_sum, shift_sum, w_in_sum, b...  89.8 us
    psum x1, blocking collectives, local(): lax.psum(lax.psum((kernel_sum, bias_sum, gain_sum, shift_sum, w_in_sum, b...  42.8 us
    another operation x1, other arithmetic  24.1 us
    ppermute x4, starting transfers between devices, from_behind(): lax.ppermute(value, axis, [(source, source + steps) for source in range(i...  21.9 us
  transfers between devices with their start and end apart: 10, of which 5 were waited for; matrix products, arithmetic and copies ran while one was open for 4% of the time, Pallas kernels for 0%

profile of v1, /device:TPU:1, one launch (start us, length us, event | category | flops | bytes accessed | tf_op | source)
XLA Modules:
  0.0 1024.6 jit_solution(15034810615370859510)
XLA Ops:
  8.4 4.6 collective-permute-start
  13.0 5.5 collective-permute-start.1
  20.7 8.0 collective-permute-start.2
  32.9 7.4 collective-permute-done.3
  40.5 4.3 fusion.223
  45.6 1.7 fusion.107
  47.4 2.0 convert_reduce_fusion
  51.9 1.9 fusion.203
  53.9 1.9 fusion.153
  56.9 24.1 %fusion.221 = (bf16[96,14,134]{2,1,0:T(8,128)(2,1)}, f32[96,14,134]{2,1,0:T(8,128)S(1)}) fusion(f32[96]{0:T(128)S(1)} %get-tuple-element.154, f32[96]{0:T(128)S(1)} %get-tuple-element.173, f32[96]{0:T(128)S(1)} %copy-done.31, f32[96]{0:T(128)S(1)} %copy-done.47, f32[96]{0:T(128)S(1)} %copy-done.45, f32[96]{0:T(128)S(1)} %copy-done.43, f32[96]{0:T(128)S(1)} %copy-done.41, ...), kind=kLoop, calls=%fused_computation.460 | loop fusion | flops 17649408 | bytes 1492608 | tf_op jit(solution)/shard_map/convert.3
  84.1 2.9 stack.199
  87.1 1.8 fusion.206
  89.0 260.9 %all-reduce.1 = (f32[96,7,7]{0,2,1:T(8,128)S(1)}, f32[96]{0:T(128)S(1)}, f32[96]{0:T(128)S(1)}, f32[96]{0:T(128)S(1)}, f32[384]{0:T(512)S(1)}, /*index=5*/f32[96]{0:T(128)S(1)}) all-reduce(f32[96,7,7]{0,2,1:T(8,128)S(1)} %reshape.203, f32[96]{0:T(128)S(1)} %copy-done.55, ...), channel_id=1, replica_groups=mesh['col'=64,'row'=8] {'col'}, use_global_device_ids=true, to_apply=%region_53.54 | all-reduce | flops 5472 | bytes 43776 | tf_op jit(solution)/shard_map/psum | solution.py:130
  349.9 42.8 %all-reduce.3 = (f32[96,7,7]{0,2,1:T(8,128)S(1)}, f32[96]{0:T(128)S(1)}, f32[96]{0:T(128)S(1)}, f32[96]{0:T(128)S(1)}, f32[384]{0:T(512)S(1)}, /*index=5*/f32[96]{0:T(128)S(1)}) all-reduce(f32[96,7,7]{0,2,1:T(8,128)S(1)} %get-tuple-element.121, f32[96]{0:T(128)S(1)} %get-tuple-element.122, ...), channel_id=1, replica_groups=mesh['col'=64,'row'=8] {'row'}, use_global_device_ids=true, to_apply=%region_54.55 | all-reduce | flops 5472 | bytes 43776 | tf_op jit(solution)/shard_map/psum | solution.py:129
  395.1 3.9 collective-permute-start.4
  401.8 2.6 scatter-add.14
  404.4 5.7 collective-permute-done.5
  411.1 2.6 scatter-add.15
  413.9 10.5 %collective-permute-start.6 = (f32[96,8,3]{2,1,0:T(8,128)S(1)}, f32[96,8,3]{2,1,0:T(8,128)S(1)}, u32[]{:S(2)}, u32[]{:S(2)}) collective-permute-start(f32[96,8,3]{2,1,0:T(8,128)S(1)} %get-tuple-element.143), channel_id=1, source_target_pairs={{0,8},{8,16},{16,24},{24,32},{32,40},{40,48},{48,56},{56,64},{64,7... | collective-permute-start | bytes 27656 | tf_op jit(solution)/shard_map/ppermute | solution.py:24
  425.8 6.2 collective-permute-start.7
  432.2 6.1 scatter-add.16
  438.3 467.0 %all-reduce.8.cloned.1.call-done = (f32[96,384]{1,0:T(8,128)}, f32[384,96]{0,1:T(8,128)}) async-done(((f32[96,384]{1,0:T(8,128)}, f32[384,96]{0,1:T(8,128)}), (f32[96,384]{1,0:T(8,128)}, f32[384,96]{0,1:T(8,128)})) %all-reduce.8.cloned.1.call-update) | async-done | bytes 294928 | tf_op jit(solution)/shard_map/psum | solution.py:130
  905.5 18.6 %scatter-add.19 = f32[96,8,128]{2,1,0:T(8,128)S(1)} dynamic-update-slice(f32[96,8,128]{2,1,0:T(8,128)S(1)} %scatter-add.16, f32[96,8,3]{2,1,0:T(8,128)S(1)} %slice_add_fusion, s32[]{:T(128)} %constant.134.clone.1, s32[]{:T(128)} %constant.134.clone.1, s32[]{:T(128)} %constant.136.clone.1) | dynamic-update-slice | bytes 18436 | tf_op jit(solution)/shard_map/scatter-add | solution.py:125
  924.8 89.8 %all-reduce.10.cloned.1.call-done = (f32[96,384]{1,0:T(8,128)}, f32[384,96]{0,1:T(8,128)}) async-done(((f32[96,384]{1,0:T(8,128)}, f32[384,96]{0,1:T(8,128)}), (f32[96,384]{1,0:T(8,128)}, f32[384,96]{0,1:T(8,128)})) %all-reduce.10.cloned.1.call-update) | async-done | bytes 294928 | tf_op jit(solution)/shard_map/psum | solution.py:129
  (228 shorter events, 26.4 us)
Async XLA Ops:
  7.2 38.4 %copy-start = (bf16[96,384]{1,0:T(8,128)(2,1)S(1)}, bf16[96,384]{1,0:T(8,128)(2,1)}, u32[]{:S(2)}) copy-start(bf16[96,384]{1,0:T(8,128)(2,1)} %param.24) | copy-start | bytes 221188
  7.2 898.1 %all-reduce.8.cloned.1.call-start = ((), (), s32[]{:S(2)}) async-start(), calls=%async_computation | async-start | bytes 589824 | tf_op jit(solution)/shard_map/psum | solution.py:130
  8.4 32.1 %copy-start.84 = (f32[96]{0:T(128)S(1)}, f32[96]{0:T(128)}, u32[]{:S(2)}) copy-start(f32[96]{0:T(128)} %param.21) | copy-start | bytes 1156
  8.4 12.2 %collective-permute-start = (bf16[96,8,3]{0,2,1:T(4,128)(2,1)S(1)}, bf16[96,8,3]{0,2,1:T(4,128)(2,1)S(1)}, u32[]{:S(2)}, u32[]{:S(2)}) collective-permute-start(bf16[96,8,3]{0,2,1:T(4,128)(2,1)S(1)} %get-tuple-element.152), channel_id=1, source_target_pairs={{0,8},{8,16},{16,24},{24,32},{32,40},{40,48},{48,56},{56,64},{64,7... | collective-permute-start | bytes 13832 | tf_op jit(solution)/shard_map/ppermute | solution.py:13
  13.0 7.6 collective-permute-start.1
  20.5 24.3 %copy-start.10 = (f32[96]{0:T(128)}, f32[96]{0:T(128)S(1)}, u32[]{:S(2)}) copy-start(f32[96]{0:T(128)S(1)} %get-tuple-element.182) | copy-start | bytes 1156
  20.5 24.3 %copy-start.12 = (f32[96]{0:T(128)}, f32[96]{0:T(128)S(1)}, u32[]{:S(2)}) copy-start(f32[96]{0:T(128)S(1)} %get-tuple-element.183) | copy-start | bytes 1156
  20.5 24.3 %copy-start.14 = (f32[96]{0:T(128)}, f32[96]{0:T(128)S(1)}, u32[]{:S(2)}) copy-start(f32[96]{0:T(128)S(1)} %get-tuple-element.184) | copy-start | bytes 1156
  20.5 24.3 %copy-start.16 = (f32[96]{0:T(128)}, f32[96]{0:T(128)S(1)}, u32[]{:S(2)}) copy-start(f32[96]{0:T(128)S(1)} %get-tuple-element.185) | copy-start | bytes 1156
  20.5 24.3 %copy-start.18 = (f32[96]{0:T(128)}, f32[96]{0:T(128)S(1)}, u32[]{:S(2)}) copy-start(f32[96]{0:T(128)S(1)} %get-tuple-element.186) | copy-start | bytes 1156
  20.5 24.3 %copy-start.20 = (f32[96]{0:T(128)}, f32[96]{0:T(128)S(1)}, u32[]{:S(2)}) copy-start(f32[96]{0:T(128)S(1)} %get-tuple-element.187) | copy-start | bytes 1156
  20.5 24.3 %copy-start.22 = (f32[96]{0:T(128)}, f32[96]{0:T(128)S(1)}, u32[]{:S(2)}) copy-start(f32[96]{0:T(128)S(1)} %get-tuple-element.188) | copy-start | bytes 1156
  20.5 24.3 %copy-start.24 = (f32[96]{0:T(128)}, f32[96]{0:T(128)S(1)}, u32[]{:S(2)}) copy-start(f32[96]{0:T(128)S(1)} %get-tuple-element.189) | copy-start | bytes 1156
  20.6 24.3 %copy-start.26 = (f32[96]{0:T(128)}, f32[96]{0:T(128)S(1)}, u32[]{:S(2)}) copy-start(f32[96]{0:T(128)S(1)} %get-tuple-element.190) | copy-start | bytes 1156
  20.6 24.3 %copy-start.28 = (f32[96]{0:T(128)}, f32[96]{0:T(128)S(1)}, u32[]{:S(2)}) copy-start(f32[96]{0:T(128)S(1)} %get-tuple-element.191) | copy-start | bytes 1156
  20.7 12.2 %collective-permute-start.2 = (bf16[96,3,134]{0,2,1:T(8,128)(2,1)S(1)}, bf16[96,3,134]{0,2,1:T(8,128)(2,1)S(1)}, u32[]{:S(2)}, u32[]{:S(2)}) collective-permute-start(bf16[96,3,134]{0,2,1:T(8,128)(2,1)S(1)} %get-tuple-element.150), channel_id=1, source_target_pairs={{0,1},{1,2},{2,3},{3,4},{4,5},{5,6},{6,7},{8,9},{9,10},{10,11},{11... | collective-permute-start | bytes 231560 | tf_op jit(solution)/shard_map/ppermute | solution.py:13
  28.7 11.6 %collective-permute-start.3 = (bf16[96,3,134]{0,2,1:T(8,128)(2,1)S(1)}, bf16[96,3,134]{0,2,1:T(8,128)(2,1)S(1)}, u32[]{:S(2)}, u32[]{:S(2)}) collective-permute-start(bf16[96,3,134]{0,2,1:T(8,128)(2,1)S(1)} %get-tuple-element.151), channel_id=1, source_target_pairs={{1,0},{2,1},{3,2},{4,3},{5,4},{6,5},{7,6},{9,8},{10,9},{11,10},{12... | collective-permute-start | bytes 231560 | tf_op jit(solution)/shard_map/ppermute | solution.py:16
  83.8 311.2 %copy-start.6 = (bf16[96,14,134]{2,1,0:T(8,128)(2,1)S(1)}, bf16[96,14,134]{2,1,0:T(8,128)(2,1)}, u32[]{:S(2)}) copy-start(bf16[96,14,134]{2,1,0:T(8,128)(2,1)} %get-tuple-element.137) | copy-start | bytes 1080580
  395.1 6.5 collective-permute-start.4
  399.6 10.4 %collective-permute-start.5 = (bf16[96,3,134]{2,1,0:T(4,128)(2,1)S(1)}, bf16[96,3,134]{2,1,0:T(4,128)(2,1)}, u32[]{:S(2)}, u32[]{:S(2)}) collective-permute-start(bf16[96,3,134]{2,1,0:T(4,128)(2,1)S(1)} %get-tuple-element.144), channel_id=1, source_target_pairs={{1,0},{2,1},{3,2},{4,3},{5,4},{6,5},{7,6},{9,8},{10,9},{11,10},{12... | collective-permute-start | bytes 231560 | tf_op jit(solution)/shard_map/ppermute | solution.py:24
  401.0 613.6 %all-reduce.10.cloned.1.call-start = ((), (), s32[]{:S(2)}) async-start(), calls=%async_computation.1 | async-start | bytes 589824 | tf_op jit(solution)/shard_map/psum | solution.py:129
  413.9 18.1 %collective-permute-start.6 = (f32[96,8,3]{2,1,0:T(8,128)S(1)}, f32[96,8,3]{2,1,0:T(8,128)S(1)}, u32[]{:S(2)}, u32[]{:S(2)}) collective-permute-start(f32[96,8,3]{2,1,0:T(8,128)S(1)} %get-tuple-element.143), channel_id=1, source_target_pairs={{0,8},{8,16},{16,24},{24,32},{32,40},{40,48},{48,56},{56,64},{64,7... | collective-permute-start | bytes 27656 | tf_op jit(solution)/shard_map/ppermute | solution.py:24
  425.8 479.5 %collective-permute-start.7 = (f32[96,8,3]{2,1,0:T(8,128)S(1)}, f32[96,8,3]{2,1,0:T(8,128)S(1)}, u32[]{:S(2)}, u32[]{:S(2)}) collective-permute-start(f32[96,8,3]{2,1,0:T(8,128)S(1)} %get-tuple-element.142), channel_id=1, source_target_pairs={{8,0},{16,8},{24,16},{32,24},{40,32},{48,40},{56,48},{64,56},{72,6... | collective-permute-start | bytes 27656 | tf_op jit(solution)/shard_map/ppermute | solution.py:24
  432.2 491.9 %copy-start.7 = (bf16[96,8,128]{2,1,0:T(8,128)(2,1)S(1)}, bf16[96,8,128]{2,1,0:T(8,128)(2,1)}, u32[]{:S(2)}) copy-start(bf16[96,8,128]{2,1,0:T(8,128)(2,1)} %param.19) | copy-start | bytes 589828
  (73 other events, 399.4 us)
Sparse Core Ops, SparseCore 0:
  401.1 504.1 all-reduce.7
  908.6 105.9 all-reduce.9
